TPU v7x, 256 devices: a whole 4x4x8 slice. The times are simulated.
256 devices in a mesh: seq: 32 (over z, y), tp: 8 (over x, core).
Axes of the slice: x: 4, y: 4, z: 8, core: 2. Of those that a mesh axis runs over, the one named last changes fastest.
Arguments:
- embedded: bfloat16 [32, 4, 1536], replicated, may hold values from -45 to 45
- lengths: int32 [32], replicated, may hold values from 1 to 32768, 524288 in all
- routes: int32 [128, 8], replicated, may hold values from 0 to 39, all different within a row; in each aligned block of 128 rows (0 to 127, 128 to 255, ...) at most 64 rows name the same one
- attn_gain: float32 [1536], replicated, may hold values from 0.1 to 1.9
- query_key_value_weight: bfloat16 [1536, 8, 320], P(None, 'tp'), may hold values from -0.15625 to 0.15625
- cache_k: bfloat16 [32, 8, 32768, 64], P(None, 'tp', 'seq'), may hold values from -350 to 350
- value_cache: bfloat16 [32, 8, 32768, 64], P(None, 'tp', 'seq'), may hold values from -6 to 6
- output_weight: bfloat16 [8, 192, 1536], P('tp'), may hold values from -0.75 to 0.75
- moe_gain: float32 [1536], replicated, may hold values from 0.1 to 1.9
- w_router: bfloat16 [1536, 40], P('seq'), may hold values from -13 to 13
- w_gate_up: bfloat16 [40, 1536, 2, 512], P('tp', 'seq'), may hold values from -0.15625 to 0.15625
- w_down: bfloat16 [40, 1536, 512], P('tp', 'seq'), may hold values from -0.25 to 0.25
Outputs:
- result: bfloat16 [128, 1536], P('tp', 'seq')
Inputs may be any that keep to these rules, and one draw needn't show every extreme that they name: `lengths`: the positions below a request's length hold its earlier keys and values; the longest request fills all 32768 positions. `routes`: each token names 8 distinct experts; over all 128 tokens no expert is named more than 64 times, a bound that some block reaches.
All inputs are finite; a program needn't handle non-finite values.
Results may differ from a plain program's by a relative error of at most 0.035.
Values may be sent and summed in bfloat16 or wider, within the bound.
No kernel may reach another device: no remote copies, remote signals or barrier semaphores. Data moves between devices by JAX's collectives and lax.ppermute only.
A program may use at most 64 MiB of HBM per device.

v0:
```python
import jax
import jax.numpy as jnp
from jax import lax
from jax.sharding import PartitionSpec as P

EPSILON = 1e-06
ROPE_BASE = 10000.0
SCORE_SCALE = 0.125
NEG_LARGE = -1e30


def rotate(values, angles):
    half = values.shape[-1] // 2
    cosine = jnp.cos(angles)
    sine = jnp.sin(angles)
    front = values[..., :half]
    back = values[..., half:]
    return jnp.concatenate([front * cosine - back * sine, back * cosine + front * sine], axis=-1)


def join_partials(first, second_half):
    top_first, total_first, sum_first = first
    top_second, total_second, sum_second = second_half
    highest = jnp.maximum(top_first, top_second)
    scale_first = jnp.exp(top_first - highest)
    scale_second = jnp.exp(top_second - highest)
    totals = total_first * scale_first + total_second * scale_second
    sums = sum_first * scale_first[..., None] + sum_second * scale_second[..., None]
    return (highest, totals, sums)


def per_device(
    embedded,
    lengths,
    routes,
    attn_gain,
    query_key_value_weight,
    cache_k,
    value_cache,
    output_weight,
    moe_gain,
    w_router,
    w_gate_up,
    w_down,
):
    requests, new_count, width = embedded.shape
    token_count = requests * new_count
    heads_here = query_key_value_weight.shape[1]
    head_extent = cache_k.shape[3]
    head_groups = query_key_value_weight.shape[2] // head_extent - 2
    ctx_here = cache_k.shape[2]
    part_width = w_router.shape[0]
    seq_index = lax.axis_index("seq")
    tp_index = lax.axis_index("tp")
    inputs = embedded.astype(jnp.float32)
    stat = jnp.mean(inputs * inputs, axis=-1, keepdims=True)
    normed = (inputs * lax.rsqrt(stat + EPSILON) * attn_gain).astype(jnp.bfloat16)
    projected_rows = jnp.einsum(
        "rtd,dhc->rthc", normed, query_key_value_weight, preferred_element_type=jnp.float32
    )
    split_parts = projected_rows.reshape(
        requests, new_count, heads_here, head_groups + 2, head_extent
    )
    half = head_extent // 2
    freqs = ROPE_BASE ** (-jnp.arange(half, dtype=jnp.float32) / half)
    positions = (
        lengths.astype(jnp.float32)[:, None] + jnp.arange(new_count, dtype=jnp.float32)[None, :]
    )
    angles = positions[:, :, None] * freqs
    queries = rotate(split_parts[:, :, :, :head_groups], angles[:, :, None, None, :]).astype(
        jnp.bfloat16
    )
    new_keys = rotate(split_parts[:, :, :, head_groups], angles[:, :, None, :]).astype(jnp.bfloat16)
    new_values = split_parts[:, :, :, head_groups + 1].astype(jnp.bfloat16)
    scores = (
        jnp.einsum("rthqe,rhpe->rhqtp", queries, cache_k, preferred_element_type=jnp.float32)
        * SCORE_SCALE
    )
    places = seq_index * ctx_here + jnp.arange(ctx_here, dtype=jnp.int32)
    live = (places[None, :] < lengths[:, None])[:, None, None, None, :]
    masked = jnp.where(live, scores, NEG_LARGE)
    local_top = jnp.max(masked, axis=-1)
    global_top = lax.pmax(local_top, "seq")
    probs = jnp.where(live, jnp.exp(masked - global_top[..., None]), 0.0)
    totals = jnp.sum(probs, axis=-1)
    sums = jnp.einsum(
        "rhqtp,rhpe->rhqte",
        probs.astype(jnp.bfloat16),
        value_cache,
        preferred_element_type=jnp.float32,
    )
    totals, sums = lax.psum((totals, sums), "seq")
    cache_part = (global_top, totals, sums)
    new_scores = (
        jnp.einsum("rthqe,rshe->rhqts", queries, new_keys, preferred_element_type=jnp.float32)
        * SCORE_SCALE
    )
    newest = jnp.arange(new_count, dtype=jnp.int32)
    causal = newest[None, :] <= newest[:, None]
    new_masked = jnp.where(causal, new_scores, NEG_LARGE)
    new_top = jnp.max(new_masked, axis=-1)
    new_probs = jnp.where(causal, jnp.exp(new_masked - new_top[..., None]), 0.0)
    new_sums = jnp.einsum(
        "rhqts,rshe->rhqte",
        new_probs.astype(jnp.bfloat16),
        new_values,
        preferred_element_type=jnp.float32,
    )
    joined_top, joined_totals, joined_sums = join_partials(
        cache_part, (new_top, jnp.sum(new_probs, axis=-1), new_sums)
    )
    attention_result = (joined_sums / joined_totals[..., None]).astype(jnp.bfloat16)
    flattened_rows = jnp.transpose(attention_result, (0, 3, 1, 2, 4)).reshape(
        token_count, heads_here, head_groups * head_extent
    )
    rows_in = inputs.reshape(token_count, width)
    attn_rows = jnp.einsum(
        "nhc,hcd->nd", flattened_rows, output_weight, preferred_element_type=jnp.float32
    )
    attn_rows = lax.psum(attn_rows, "tp")
    whole_rows = rows_in + attn_rows
    row_scale = lax.rsqrt(jnp.mean(whole_rows * whole_rows, axis=-1, keepdims=True) + EPSILON)
    residual = lax.dynamic_slice_in_dim(whole_rows, seq_index * part_width, part_width, 1)
    gain_part = lax.dynamic_slice_in_dim(moe_gain, seq_index * part_width, part_width, 0)
    mixed_rows = (residual * row_scale * gain_part).astype(jnp.bfloat16)
    experts_here = w_gate_up.shape[0]
    expert_count = experts_here * lax.axis_size("tp")
    top_count = routes.shape[1]
    capacity = token_count // 2
    flat_routes = routes.reshape(-1)
    onehot = (flat_routes[:, None] == jnp.arange(expert_count, dtype=jnp.int32)[None, :]).astype(
        jnp.int32
    )
    slots = jnp.sum((jnp.cumsum(onehot, axis=0) - onehot) * onehot, axis=1).reshape(
        token_count, top_count
    )
    local_ids = tp_index * experts_here + jnp.arange(experts_here, dtype=jnp.int32)
    slot_ids = jnp.arange(capacity, dtype=jnp.int32)
    hits = (routes[None, None] == local_ids[:, None, None, None]) & (
        slots[None, None] == slot_ids[None, :, None, None]
    )
    dispatch = jnp.any(hits, axis=-1)
    expert_in = jnp.einsum(
        "ecn,nd->ecd", dispatch.astype(jnp.bfloat16), mixed_rows, preferred_element_type=jnp.float32
    ).astype(jnp.bfloat16)
    both_part = jnp.einsum(
        "ecd,edgh->ecgh", expert_in, w_gate_up, preferred_element_type=jnp.float32
    )
    logit_part = jnp.dot(mixed_rows, w_router, preferred_element_type=jnp.float32)
    both, logits = lax.psum((both_part, logit_part), "seq")
    choose = routes[:, :, None] == jnp.arange(expert_count, dtype=jnp.int32)[None, None, :]
    picked = jnp.sum(jnp.where(choose, logits[:, None, :], 0.0), axis=-1)
    combine = jax.nn.softmax(picked, axis=-1)
    slot_weight = jnp.sum(jnp.where(hits, combine[None, None], 0.0), axis=(2, 3))
    hidden = (jax.nn.silu(both[:, :, 0]) * both[:, :, 1] * slot_weight[..., None]).astype(
        jnp.bfloat16
    )
    expert_out = jnp.einsum("ech,edh->ecd", hidden, w_down, preferred_element_type=jnp.float32)
    moe_part = jnp.einsum(
        "ecn,ecd->nd", dispatch.astype(jnp.float32), expert_out, precision=lax.Precision.HIGHEST
    )
    row_count = token_count // lax.axis_size("tp")
    moe_rows = lax.psum_scatter(moe_part, "tp", scatter_dimension=0, tiled=True)
    base_rows = lax.dynamic_slice_in_dim(residual, tp_index * row_count, row_count, 0)
    return (base_rows + moe_rows).astype(jnp.bfloat16)


def solution(mesh):
    in_specs = (
        P(),
        P(),
        P(),
        P(),
        P(None, "tp", None),
        P(None, "tp", "seq", None),
        P(None, "tp", "seq", None),
        P("tp", None, None),
        P(),
        P("seq", None),
        P("tp", "seq", None, None),
        P("tp", "seq", None),
    )
    out_specs = P("tp", "seq")
    return jax.shard_map(
        per_device, mesh=mesh, in_specs=in_specs, out_specs=out_specs, check_vma=False
    )
```

profile of v0, /device:TPU:1, one launch (start us, length us, event | category | flops | bytes accessed | tf_op | source)
XLA Modules:
  0.0 574.5 jit_solution(12044769910729706812)
XLA Ops:
  6.6 0.7 convert_element_type.57
  7.3 1.4 multiply_reduce_fusion.1
  8.8 0.7 broadcast_compare_fusion
  9.5 0.3 multiply_cosine_fusion.1
  9.8 1.3 fusion.33
  11.1 0.6 convolution_bitcast_fusion
  12.0 1.2 fusion.80
  13.2 118.9 %pmax.7 = f32[32,1,3,4]{3,2,0,1:T(4,128)S(1)} all-reduce(f32[32,1,3,4]{3,2,0,1:T(4,128)S(1)} %bitcast.166), channel_id=1, replica_groups=mesh['seq'=32,'tp'=8] {'seq'}, use_global_device_ids=true, to_apply=%region_2.3 | all-reduce | flops 384 | bytes 3072 | tf_op jit(solution)/shard_map/pmax | solution.py:83
  132.1 4.3 fusion.8
  136.5 1.0 fusion.19
  137.7 11.3 %reduce-window.6 = s32[40,8,128]{2,1,0:T(8,128)S(1)} reduce-window(s32[40,8,128]{2,1,0:T(8,128)S(1)} %fusion.40, s32[]{:T(128)} %constant.56.clone.1), window={size=1x1x128 pad=0_0x0_0x127_0}, to_apply=%region_9.10 | reduce-window | flops 5201920 | bytes 327684 | tf_op jit(solution)/shard_map/reduce-window
  149.4 0.3 fusion.71
  149.7 110.4 %psum.36 = f32[32,1,3,4]{3,2,0,1:T(4,128)S(1)} all-reduce(f32[32,1,3,4]{3,2,0,1:T(4,128)S(1)} %bitcast.167), channel_id=1, replica_groups=mesh['seq'=32,'tp'=8] {'seq'}, use_global_device_ids=true, to_apply=%region_6.7 | all-reduce | flops 384 | bytes 3072 | tf_op jit(solution)/shard_map/psum | solution.py:92
  260.3 0.8 fusion.81
  261.0 0.2 fusion.41
  261.5 37.6 %all-reduce.4.cloned.1.call-done = f32[32,1,3,4,64]{4,3,2,0,1:T(4,128)} async-done(((f32[32,1,3,4,64]{4,3,2,0,1:T(4,128)}), f32[32,1,3,4,64]{4,3,2,0,1:T(4,128)}) %all-reduce.4.cloned.1.call-update) | async-done | bytes 98320 | tf_op jit(solution)/shard_map/psum | solution.py:92
  299.0 1.5 fusion.16
  300.6 0.1 reshape.268
  300.8 1.2 fusion.29
  302.3 0.8 dynamic_slice.11
  303.1 0.4 and_reduce_fusion
  303.6 75.7 %all-reduce.6.cloned.1.call-done = f32[128,1536]{1,0:T(8,128)} async-done(((f32[128,1536]{1,0:T(8,128)}), f32[128,1536]{1,0:T(8,128)}) %all-reduce.6.cloned.1.call-update) | async-done | bytes 786448 | tf_op jit(solution)/shard_map/psum | solution.py:120
  379.2 1.3 multiply_reduce_fusion
  380.6 1.7 fusion.31
  382.4 0.2 fusion.79
  382.6 115.7 %psum.39 = f32[128,40]{0,1:T(8,128)S(1)} all-reduce(f32[128,40]{0,1:T(8,128)S(1)} %fusion.79), channel_id=1, replica_groups=mesh['seq'=32,'tp'=8] {'seq'}, use_global_device_ids=true, to_apply=%region_15.16 | all-reduce | flops 5120 | bytes 40960 | tf_op jit(solution)/shard_map/psum | solution.py:150
  498.4 0.7 fusion.7
  499.2 31.7 %all-reduce.8.cloned.1.call-done = f32[5,64,2,512]{3,1,2,0:T(8,128)} async-done(((f32[5,64,2,512]{3,1,2,0:T(8,128)}), f32[5,64,2,512]{3,1,2,0:T(8,128)}) %all-reduce.8.cloned.1.call-update) | async-done | bytes 1310736 | tf_op jit(solution)/shard_map/psum | solution.py:150
  530.9 1.6 fusion.35
  532.5 1.0 convolution_bitcast_fusion.1
  533.5 33.1 %reduce-scatter.2.cloned.1.call-done = f32[16,48]{1,0:T(8,128)} async-done(((f32[128,48]{1,0:T(8,128)}), f32[16,48]{1,0:T(8,128)}) %reduce-scatter.2.cloned.1.call-update) | async-done | bytes 3088 | tf_op jit(solution)/shard_map/reduce_scatter | solution.py:163
  566.6 1.4 add_convert_fusion.1
  (58 shorter events, 1.9 us)
Async XLA Ops:
  6.5 4.6 copy-start
  6.5 292.5 %all-reduce.4.cloned.1.call-start = ((), (), s32[]{:S(2)}) async-start(), calls=%async_computation.1 | async-start | bytes 393216 | tf_op jit(solution)/shard_map/psum | solution.py:92
  7.3 4.7 copy-start.1
  136.3 1.1 copy-start.5
  136.4 242.9 %all-reduce.6.cloned.1.call-start = ((), (), s32[]{:S(2)}) async-start(), calls=%async_computation.2 | async-start | bytes 1572864 | tf_op jit(solution)/shard_map/psum | solution.py:120
  299.0 1.7 copy-start.3
  300.5 1.5 copy-start.2
  301.9 228.9 %all-reduce.8.cloned.1.call-start = ((), (), s32[]{:S(2)}) async-start(), calls=%async_computation.3 | async-start | bytes 2621440 | tf_op jit(solution)/shard_map/psum | solution.py:150
  302.1 78.5 %copy-start.4 = (bf16[5,48,2,512]{3,2,1,0:T(2,128)(2,1)S(1)}, bf16[5,48,2,512]{3,2,1,0:T(2,128)(2,1)}, u32[]{:S(2)}) copy-start(bf16[5,48,2,512]{3,2,1,0:T(2,128)(2,1)} %param.22) | copy-start | bytes 1474564
  380.6 1.8 copy-start.6
  380.6 150.3 %copy-start.7 = (bf16[5,48,512]{2,1,0:T(8,128)(2,1)S(1)}, bf16[5,48,512]{2,1,0:T(8,128)(2,1)}, u32[]{:S(2)}) copy-start(bf16[5,48,512]{2,1,0:T(8,128)(2,1)} %param.23) | copy-start | bytes 737284
  382.4 184.3 %reduce-scatter.2.cloned.1.call-start = ((), (), s32[]{:S(2)}) async-start(), calls=%async_computation.4 | async-start | bytes 73728 | tf_op jit(solution)/shard_map/reduce_scatter | solution.py:163
Sparse Core Ops, SparseCore 0:
  136.5 162.5 all-reduce.3
  302.1 77.1 all-reduce.5
  382.7 148.1 all-reduce.7
  533.7 32.9 reduce-scatter.1
where the time goes:
time: 576 us; the launch traced here: 575 us
  blocking collectives  345 us (60%)
  waiting for transfers between devices  178 us (31%)
  other arithmetic  22 us (4%)
  matrix products  14 us (2%)
  between operations  13.4 us (2%)
    pmax x1, blocking collectives, per_device(): global_top = lax.pmax(local_top, 'seq')  119 us
    psum x1, blocking collectives, per_device(): both, logits = lax.psum((both_part, logit_part), 'seq')  116 us
    psum x1, blocking collectives, per_device(): totals, sums = lax.psum((totals, sums), 'seq')  110 us
    psum x1, waiting for transfers between devices, per_device(): attn_rows = lax.psum(attn_rows, 'tp')  75.7 us
    psum x1, waiting for transfers between devices, per_device(): totals, sums = lax.psum((totals, sums), 'seq')  37.6 us
    reduce_scatter x1, waiting for transfers between devices, per_device(): moe_rows = lax.psum_scatter(moe_part, 'tp', scatter_dimension=0, tiled=True)  33.1 us
    psum x1, waiting for transfers between devices, per_device(): both, logits = lax.psum((both_part, logit_part), 'seq')  31.7 us
  transfers between devices with their start and end apart: 4, of which 4 were waited for; matrix products, arithmetic and copies ran while one was open for 3% of the time, Pallas kernels for 0%

commit v1 on v0

v1 whole, which is shorter than its diff:
```python
import jax
import jax.numpy as jnp
from jax import lax
from jax.sharding import PartitionSpec as P

EPSILON = 1e-06
ROPE_BASE = 10000.0
SCORE_SCALE = 0.125
NEG_LARGE = -1e30


def rotate(values, angles):
    half = values.shape[-1] // 2
    cosine = jnp.cos(angles)
    sine = jnp.sin(angles)
    front = values[..., :half]
    back = values[..., half:]
    return jnp.concatenate([front * cosine - back * sine, back * cosine + front * sine], axis=-1)


def butterfly_sum(values, axis):
    count = lax.axis_size(axis)
    step = 1
    while step < count:
        pairs = [(i, i ^ step) for i in range(count)]
        values = values + lax.ppermute(values, axis, pairs)
        step *= 2
    return values


def per_device(
    embedded,
    lengths,
    routes,
    attn_gain,
    query_key_value_weight,
    cache_k,
    value_cache,
    output_weight,
    moe_gain,
    w_router,
    w_gate_up,
    w_down,
):
    requests, new_count, width = embedded.shape
    token_count = requests * new_count
    head_extent = cache_k.shape[3]
    head_groups = query_key_value_weight.shape[2] // head_extent - 2
    ctx_here = cache_k.shape[2]
    part_width = w_router.shape[0]
    seq_size = lax.axis_size("seq")
    tp_size = lax.axis_size("tp")
    seq_index = lax.axis_index("seq")
    tp_index = lax.axis_index("tp")
    own_request = seq_index * (requests // seq_size)

    inputs = embedded.astype(jnp.float32)
    stat = jnp.mean(inputs * inputs, axis=-1, keepdims=True)
    normed = (inputs * lax.rsqrt(stat + EPSILON) * attn_gain).astype(jnp.bfloat16)
    projected_rows = jnp.einsum(
        "rtd,dhc->rthc", normed, query_key_value_weight, preferred_element_type=jnp.float32
    )
    split_parts = projected_rows.reshape(requests, new_count, 1, head_groups + 2, head_extent)
    half = head_extent // 2
    freqs = ROPE_BASE ** (-jnp.arange(half, dtype=jnp.float32) / half)
    positions = (
        lengths.astype(jnp.float32)[:, None] + jnp.arange(new_count, dtype=jnp.float32)[None, :]
    )
    angles = positions[:, :, None] * freqs
    queries = rotate(split_parts[:, :, :, :head_groups], angles[:, :, None, None, :]).astype(
        jnp.bfloat16
    )
    new_keys = rotate(split_parts[:, :, :, head_groups], angles[:, :, None, :]).astype(jnp.bfloat16)
    new_values = split_parts[:, :, :, head_groups + 1].astype(jnp.bfloat16)

    with jax.named_scope("cache_attention"):
        scores = (
            jnp.einsum("rthqe,rhpe->rhqtp", queries, cache_k, preferred_element_type=jnp.float32)
            * SCORE_SCALE
        )
        places = seq_index * ctx_here + jnp.arange(ctx_here, dtype=jnp.int32)
        live = (places[None, :] < lengths[:, None])[:, None, None, None, :]
        masked = jnp.where(live, scores, NEG_LARGE)
        local_top = jnp.max(masked, axis=-1)
        probs = jnp.where(live, jnp.exp(masked - local_top[..., None]), 0.0)
        totals = jnp.sum(probs, axis=-1)
        sums = jnp.einsum(
            "rhqtp,rhpe->rhqte",
            probs.astype(jnp.bfloat16),
            value_cache,
            preferred_element_type=jnp.float32,
        )
    partial = jnp.concatenate([sums, totals[..., None], local_top[..., None]], axis=-1)
    partial = partial.reshape(seq_size, -1)
    router_rows = jnp.broadcast_to(
        w_router.astype(jnp.float32).reshape(1, -1), (seq_size, w_router.size)
    )
    with jax.named_scope("gather_partials"):
        received = lax.all_to_all(
            jnp.concatenate([partial, router_rows], axis=1), "seq", 0, 0, tiled=True
        )
    partial_size = partial.shape[1]
    parts = received[:, :partial_size].reshape(seq_size, head_groups, new_count, head_extent + 2)
    router_full = (
        received[:, partial_size:].reshape(seq_size * part_width, -1).astype(jnp.bfloat16)
    )

    with jax.named_scope("merge_request"):
        own_queries = lax.dynamic_index_in_dim(queries, own_request, 0, keepdims=False)[:, 0]
        own_keys = lax.dynamic_index_in_dim(new_keys, own_request, 0, keepdims=False)[:, 0]
        own_values = lax.dynamic_index_in_dim(new_values, own_request, 0, keepdims=False)[:, 0]
        new_scores = (
            jnp.einsum("tqe,se->qts", own_queries, own_keys, preferred_element_type=jnp.float32)
            * SCORE_SCALE
        )
        newest = jnp.arange(new_count, dtype=jnp.int32)
        causal = newest[None, :] <= newest[:, None]
        new_masked = jnp.where(causal, new_scores, NEG_LARGE)
        new_top = jnp.max(new_masked, axis=-1)
        new_probs = jnp.where(causal, jnp.exp(new_masked - new_top[..., None]), 0.0)
        new_sums = jnp.einsum(
            "qts,se->qte",
            new_probs.astype(jnp.bfloat16),
            own_values,
            preferred_element_type=jnp.float32,
        )
        part_sums = parts[..., :head_extent]
        part_totals = parts[..., head_extent]
        part_tops = parts[..., head_extent + 1]
        highest = jnp.maximum(jnp.max(part_tops, axis=0), new_top)
        part_scale = jnp.exp(part_tops - highest)
        new_scale = jnp.exp(new_top - highest)
        joined_totals = jnp.sum(part_totals * part_scale, axis=0) + jnp.sum(new_probs, axis=-1) * new_scale
        joined_sums = (
            jnp.sum(part_sums * part_scale[..., None], axis=0) + new_sums * new_scale[..., None]
        )
        attended = (joined_sums / joined_totals[..., None]).astype(jnp.bfloat16)
        attended = jnp.transpose(attended, (1, 0, 2)).reshape(new_count, head_groups * head_extent)
    attn_part = jnp.dot(attended, output_weight[0], preferred_element_type=jnp.float32)
    with jax.named_scope("sum_heads"):
        attn_rows = butterfly_sum(attn_part, "tp")

    own_inputs = lax.dynamic_index_in_dim(inputs, own_request, 0, keepdims=False)
    whole_rows = own_inputs + attn_rows
    row_scale = lax.rsqrt(jnp.mean(whole_rows * whole_rows, axis=-1, keepdims=True) + EPSILON)
    own_mixed = (whole_rows * row_scale * moe_gain).astype(jnp.bfloat16)
    own_logits = jnp.dot(own_mixed, router_full, preferred_element_type=jnp.float32)

    def by_column_block(values):
        return jnp.transpose(values.reshape(new_count, seq_size, part_width), (1, 0, 2))

    expert_count = own_logits.shape[1]
    outgoing = jnp.concatenate(
        [
            by_column_block(own_mixed.astype(jnp.float32)),
            by_column_block(whole_rows),
            jnp.broadcast_to(own_logits[None], (seq_size, new_count, expert_count)),
        ],
        axis=-1,
    )
    with jax.named_scope("spread_rows"):
        incoming = lax.all_to_all(outgoing, "seq", 0, 0, tiled=True)
    mixed_rows = incoming[..., :part_width].reshape(token_count, part_width).astype(jnp.bfloat16)
    residual = incoming[..., part_width : 2 * part_width].reshape(token_count, part_width)
    logits = incoming[..., 2 * part_width :].reshape(token_count, expert_count)

    experts_here = w_gate_up.shape[0]
    top_count = routes.shape[1]
    capacity = token_count // 2
    pair_count = token_count * top_count
    flat_routes = routes.reshape(-1)
    local_ids = tp_index * experts_here + jnp.arange(experts_here, dtype=jnp.int32)
    onehot = (flat_routes[:, None] == local_ids[None, :]).astype(jnp.bfloat16)
    pair_ids = jnp.arange(pair_count, dtype=jnp.int32)
    earlier = (pair_ids[None, :] < pair_ids[:, None]).astype(jnp.bfloat16)
    before = jnp.dot(earlier, onehot, preferred_element_type=jnp.float32)
    slots = jnp.sum(before * onehot.astype(jnp.float32), axis=1).astype(jnp.int32)
    slots = slots.reshape(token_count, top_count)
    picked = jnp.take_along_axis(logits, routes, axis=1)
    combine = jax.nn.softmax(picked, axis=-1)
    slot_ids = jnp.arange(capacity, dtype=jnp.int32)
    hits = (routes[None, None] == local_ids[:, None, None, None]) & (
        slots[None, None] == slot_ids[None, :, None, None]
    )
    dispatch = jnp.any(hits, axis=-1)
    slot_weight = jnp.sum(jnp.where(hits, combine[None, None], 0.0), axis=(2, 3))

    expert_in = jnp.einsum(
        "ecn,nd->ecd", dispatch.astype(jnp.bfloat16), mixed_rows, preferred_element_type=jnp.float32
    ).astype(jnp.bfloat16)
    both_part = jnp.einsum(
        "ecd,edgh->ecgh", expert_in, w_gate_up, preferred_element_type=jnp.float32
    )
    slot_total = experts_here * capacity
    slots_each = slot_total // seq_size
    both_part = both_part.reshape(seq_size, -1)
    with jax.named_scope("reduce_gate_up"):
        both_pieces = lax.all_to_all(both_part, "seq", 0, 0, tiled=True)
    both = jnp.sum(both_pieces, axis=0).reshape(slots_each, 2, -1)
    own_weight = lax.dynamic_slice_in_dim(
        slot_weight.reshape(-1), seq_index * slots_each, slots_each, 0
    )
    hidden = (jax.nn.silu(both[:, 0]) * both[:, 1] * own_weight[:, None]).astype(jnp.bfloat16)
    hid_width = hidden.shape[1]
    with jax.named_scope("gather_hidden"):
        hidden_all = lax.all_to_all(
            jnp.broadcast_to(hidden[None], (seq_size, slots_each, hid_width)),
            "seq",
            0,
            0,
            tiled=True,
        )
    hidden_all = hidden_all.reshape(experts_here, capacity, hid_width)
    expert_out = jnp.einsum(
        "ech,edh->ecd", hidden_all, w_down, preferred_element_type=jnp.float32
    )
    moe_part = jnp.einsum(
        "ecn,ecd->nd", dispatch.astype(jnp.float32), expert_out, precision=lax.Precision.HIGHEST
    )
    row_count = token_count // tp_size
    with jax.named_scope("reduce_experts"):
        moe_pieces = lax.all_to_all(
            moe_part.reshape(tp_size, row_count, part_width), "tp", 0, 0, tiled=True
        )
    moe_rows = jnp.sum(moe_pieces, axis=0)
    base_rows = lax.dynamic_slice_in_dim(residual, tp_index * row_count, row_count, 0)
    return (base_rows + moe_rows).astype(jnp.bfloat16)


def solution(mesh):
    in_specs = (
        P(),
        P(),
        P(),
        P(),
        P(None, "tp", None),
        P(None, "tp", "seq", None),
        P(None, "tp", "seq", None),
        P("tp", None, None),
        P(),
        P("seq", None),
        P("tp", "seq", None, None),
        P("tp", "seq", None),
    )
    out_specs = P("tp", "seq")
    return jax.shard_map(
        per_device, mesh=mesh, in_specs=in_specs, out_specs=out_specs, check_vma=False
    )
```

time: 576 us -> 147 us (0.26)
  blocking collectives: 345 us -> 0 us
  waiting for transfers between devices: 178 us -> 61.3 us
  starting transfers between devices: 0.13 us -> 44 us
  local copies, waits for them, and re-layouts: 1.81 us -> 21.2 us
  between operations: 13.4 us -> 0.54 us
  other arithmetic: 22 us -> 11.9 us
  matrix products: 14 us -> 7.91 us
    psum x2 -> x0, blocking collectives: 226 us -> none  [the longest x1 116 us: per_device(): both, logits = lax.psum((both_part, logit_part), 'seq')]
    psum x3 -> x0, waiting for transfers between devices: 145 us -> none  [the longest x1 75.7 us: per_device(): attn_rows = lax.psum(attn_rows, 'tp')]
    pmax x1 -> x0, blocking collectives: 119 us -> none  [per_device(): global_top = lax.pmax(local_top, 'seq')]
    all_to_all x0 -> x5, waiting for transfers between devices: none -> 59.3 us  [the longest x1 20.8 us: per_device(): both_pieces = lax.all_to_all(both_part, 'seq', 0, 0, tiled=True)]
    all_to_all x0 -> x5, starting transfers between devices: none -> 37.6 us  [the longest x1 12 us: per_device(): lax.all_to_all(jnp.concatenate([partial, router_rows], axis=1), 'seq', 0,...]
    reduce_scatter x1 -> x0, waiting for transfers between devices: 33.1 us -> none  [per_device(): moe_rows = lax.psum_scatter(moe_part, 'tp', scatter_dimension=0, tiled=True)]
    another operation x3 -> x2, other arithmetic: 11.4 us -> 0.45 us
    gather x0 -> x5, local copies, waits for them, and re-layouts: none -> 7.39 us  [per_device(): picked = jnp.take_along_axis(logits, routes, axis=1)]
  transfers between devices with their start and end apart: 4 -> 8, of which waited for: 4 -> 8; matrix products, arithmetic and copies ran while one was open for 3% -> 8% of each run, Pallas kernels for 0% -> 0%
where the time goes in v1:
time: 147 us
  waiting for transfers between devices  61.3 us (42%)
  starting transfers between devices  44 us (30%)
  local copies, waits for them, and re-layouts  21.2 us (14%)
  other arithmetic  11.9 us (8%)
  matrix products  7.91 us (5%)
    all_to_all x1, waiting for transfers between devices, per_device(): both_pieces = lax.all_to_all(both_part, 'seq', 0, 0, tiled=True)  20.8 us
    all_to_all x1, waiting for transfers between devices, per_device(): lax.all_to_all(jnp.concatenate([partial, router_rows], axis=1), 'seq', 0,...  12.6 us
    all_to_all x1, waiting for transfers between devices, per_device(): lax.all_to_all(jnp.broadcast_to(hidden[None], (seq_size, slots_each, hid_...  12.5 us
    all_to_all x1, starting transfers between devices, per_device(): lax.all_to_all(jnp.concatenate([partial, router_rows], axis=1), 'seq', 0,...  12 us
    all_to_all x1, starting transfers between devices, per_device(): lax.all_to_all(moe_part.reshape(tp_size, row_count, part_width), 'tp', 0,...  10.8 us
    all_to_all x1, waiting for transfers between devices, per_device(): incoming = lax.all_to_all(outgoing, 'seq', 0, 0, tiled=True)  8.73 us
    gather x5, local copies, waits for them, and re-layouts, per_device(): picked = jnp.take_along_axis(logits, routes, axis=1)  7.39 us
    all_to_all x1, starting transfers between devices, per_device(): lax.all_to_all(jnp.broadcast_to(hidden[None], (seq_size, slots_each, hid_...  6.72 us
  transfers between devices with their start and end apart: 8, of which 8 were waited for; matrix products, arithmetic and copies ran while one was open for 8% of the time, Pallas kernels for 0%

profile of v1, /device:TPU:1, one launch (start us, length us, event | category | flops | bytes accessed | tf_op | source)
XLA Modules:
  0.0 146.8 jit_solution(9064611955982708827)
XLA Ops:
  0.0 0.7 convert_element_type.95
  0.8 1.3 multiply_reduce_fusion
  2.1 0.7 broadcast_compare_fusion
  3.1 1.3 fusion.32
  5.3 3.5 %fusion.82 = (f32[32,3,4]{2,1,0:T(4,128)S(1)}, f32[32,1,3,4,1024]{4,3,2,0,1:T(4,128)S(1)}) fusion(bf16[32,1,1024,64]{2,3,1,0:T(8,128)(2,1)} %param.17, bf16[32,4,3,64]{3,0,2,1:T(8,128)(2,1)S(1)} %pad_maximum_fusion.3, pred[32,1024]{1,0:T(8,128)(4,1)S(1)} %broadcast_compare_fusion), kind=kOutput, calls=%fused_computation.138 | convolution fusion | flops 51510912 | bytes 5850624 | tf_op jit(solution)/shard_map/cache_attention/rthqe,rhpe->rhqtp/dot_general | solution.py:78
  8.8 1.0 fusion.21
  9.8 1.5 %fusion.9 = f32[32,1,3,4,64]{4,3,2,0,1:T(4,128)S(1)} fusion(bf16[32,1,1024,64]{2,3,1,0:T(8,128)(2,1)S(1)} %copy-done.8, f32[32,1,3,4,1024]{4,3,2,0,1:T(4,128)S(1)} %get-tuple-element.21, f32[32,3,4]{2,1,0:T(4,128)S(1)} %get-tuple-element.20, pred[32,1024]{1,0:T(8,128)(4,1)S(1)} %broadcast_compare_fusion), kind=kOutput, calls=%fused_computation.14 | convolution fusion | flops 51511296 | bytes 5899776 | tf_op jit(solution)/shard_map/cache_attention/rhqtp,rhpe->rhqte/dot_general | solution.py:87
  11.3 0.7 copy.186
  13.4 1.0 all_to_all.23
  14.4 12.0 %all-to-all-start = ((f32[32,1,2712]{2,1,0:T(1,128)}), f32[32,1,2712]{2,1,0:T(1,128)S(1)}, u32[]{:S(2)}, u32[]{:S(2)}) async-start(f32[32,1,2712]{2,1,0:T(1,128)} %all_to_all.23), calls=%async_computation | async-start | bytes 720896 | tf_op jit(solution)/shard_map/gather_partials/all_to_all | solution.py:99
  27.2 12.6 %all-to-all-done = f32[32,1,2712]{2,1,0:T(1,128)S(1)} async-done(((f32[32,1,2712]{2,1,0:T(1,128)}), f32[32,1,2712]{2,1,0:T(1,128)S(1)}, u32[]{:S(2)}, u32[]{:S(2)}) %all-to-all-start) | async-done | bytes 347168 | tf_op jit(solution)/shard_map/gather_partials/all_to_all | solution.py:99
  41.7 2.2 %collective-permute-start = (f32[4,1536]{1,0:T(4,128)S(1)}, f32[4,1536]{1,0:T(4,128)S(1)}, u32[]{:S(2)}, u32[]{:S(2)}) collective-permute-start(f32[4,1536]{1,0:T(4,128)S(1)} %fusion.28), channel_id=1, source_target_pairs={{0,1},{1,0},{2,3},{3,2},{4,5},{5,4},{6,7},{7,6},{8,9},{9,8},{10,11... | collective-permute-start | bytes 73736 | tf_op jit(solution)/shard_map/sum_heads/ppermute | solution.py:26
  44.8 1.3 collective-permute-start.1
  46.8 0.8 collective-permute-done.1
  47.6 2.8 %collective-permute-start.2 = (f32[4,1536]{1,0:T(4,128)S(1)}, f32[4,1536]{1,0:T(4,128)S(1)}, u32[]{:S(2)}, u32[]{:S(2)}) collective-permute-start(f32[4,1536]{1,0:T(4,128)S(1)} %add.137), channel_id=1, source_target_pairs={{0,4},{1,5},{2,6},{3,7},{4,0},{5,1},{6,2},{7,3},{8,12},{9,13},{10,... | collective-permute-start | bytes 73736 | tf_op jit(solution)/shard_map/sum_heads/ppermute | solution.py:26
  52.6 0.8 pad_maximum_fusion.2
  53.5 4.2 %all-to-all-start.1 = ((f32[32,4,136]{2,1,0:T(4,128)}), f32[32,4,136]{2,1,0:T(4,128)S(1)}, u32[]{:S(2)}, u32[]{:S(2)}) async-start(f32[32,4,136]{2,1,0:T(4,128)} %pad_maximum_fusion.2), calls=%async_computation.1 | async-start | bytes 262144 | tf_op jit(solution)/shard_map/spread_rows/all_to_all | solution.py:162
  58.2 8.7 %all-to-all-done.1 = f32[32,4,136]{2,1,0:T(4,128)S(1)} async-done(((f32[32,4,136]{2,1,0:T(4,128)}), f32[32,4,136]{2,1,0:T(4,128)S(1)}, u32[]{:S(2)}, u32[]{:S(2)}) %all-to-all-start.1) | async-done | bytes 69664 | tf_op jit(solution)/shard_map/spread_rows/all_to_all | solution.py:162
  67.5 2.1 %copy.202 = f32[5,64,2,512]{3,2,1,0:T(2,128)} copy(f32[5,64,2,512]{3,1,2,0:T(8,128)S(1)} %fusion.30) | data formatting | bytes 2621440 | tf_op jit(solution)/shard_map/ecd,edgh->ecgh/dot_general | solution.py:191
  69.6 4.0 %all_to_all.31 = f32[32,1,10240]{2,1,0:T(1,128)} reshape(f32[5,64,2,512]{3,2,1,0:T(2,128)} %copy.202) | data formatting | bytes 2621440 | tf_op jit(solution)/shard_map/reduce_gate_up/all_to_all | solution.py:198
  73.6 4.0 %all-to-all-start.2 = ((f32[32,1,10240]{2,1,0:T(1,128)}), f32[32,1,10240]{2,1,0:T(1,128)S(1)}, u32[]{:S(2)}, u32[]{:S(2)}) async-start(f32[32,1,10240]{2,1,0:T(1,128)} %all_to_all.31), calls=%async_computation.2 | async-start | bytes 2621440 | tf_op jit(solution)/shard_map/reduce_gate_up/all_to_all | solution.py:198
  77.9 7.1 %gather_fusion = f32[1024]{0:T(1024)S(1)} fusion(f32[128,40]{1,0:T(8,128)S(1)} %bitcast.171, s32[1024]{0:T(1024)S(1)} %reshape.382), kind=kCustom, calls=%fused_computation | custom fusion | bytes 16384 | tf_op jit(solution)/shard_map/jit(take_along_axis)/gather | solution.py:179
  85.1 0.7 fusion.8
  86.0 20.8 %all-to-all-done.2 = f32[32,1,10240]{2,1,0:T(1,128)S(1)} async-done(((f32[32,1,10240]{2,1,0:T(1,128)}), f32[32,1,10240]{2,1,0:T(1,128)S(1)}, u32[]{:S(2)}, u32[]{:S(2)}) %all-to-all-start.2) | async-done | bytes 1310752 | tf_op jit(solution)/shard_map/reduce_gate_up/all_to_all | solution.py:198
  106.8 0.7 reduce_sum.115
  107.7 0.9 broadcast_in_dim.125
  108.6 6.7 %all-to-all-start.3 = ((bf16[32,10,512]{2,1,0:T(8,128)(2,1)}), bf16[32,10,512]{2,1,0:T(8,128)(2,1)S(1)}, u32[]{:S(2)}, u32[]{:S(2)}) async-start(bf16[32,10,512]{2,1,0:T(8,128)(2,1)} %broadcast_in_dim.125), calls=%async_computation.3 | async-start | bytes 1048576 | tf_op jit(solution)/shard_map/gather_hidden/all_to_all | solution.py:206
  115.5 12.5 %all-to-all-done.3 = bf16[32,10,512]{2,1,0:T(8,128)(2,1)S(1)} async-done(((bf16[32,10,512]{2,1,0:T(8,128)(2,1)}), bf16[32,10,512]{2,1,0:T(8,128)(2,1)S(1)}, u32[]{:S(2)}, u32[]{:S(2)}) %all-to-all-start.3) | async-done | bytes 327712 | tf_op jit(solution)/shard_map/gather_hidden/all_to_all | solution.py:206
  128.7 0.7 reshape.406
  129.4 10.8 %all-to-all-start.4 = ((f32[8,1,768]{2,1,0:T(1,128)}), f32[8,1,768]{2,1,0:T(1,128)S(1)}, u32[]{:S(2)}, u32[]{:S(2)}) async-start(f32[8,1,768]{2,1,0:T(1,128)} %reshape.406), calls=%async_computation.4 | async-start | bytes 49152 | tf_op jit(solution)/shard_map/reduce_experts/all_to_all | solution.py:222
  140.3 4.6 %all-to-all-done.4 = f32[8,1,768]{2,1,0:T(1,128)S(1)} async-done(((f32[8,1,768]{2,1,0:T(1,128)}), f32[8,1,768]{2,1,0:T(1,128)S(1)}, u32[]{:S(2)}, u32[]{:S(2)}) %all-to-all-start.4) | async-done | bytes 24608 | tf_op jit(solution)/shard_map/reduce_experts/all_to_all | solution.py:222
  145.4 0.7 reduce.4
  (108 shorter events, 12.9 us)
Async XLA Ops:
  0.0 4.4 %copy-start = (bf16[1536,1,320]{0,2,1:T(8,128)(2,1)S(1)}, bf16[1536,1,320]{0,2,1:T(8,128)(2,1)}, u32[]{:S(2)}) copy-start(bf16[1536,1,320]{0,2,1:T(8,128)(2,1)} %param.16) | copy-start | bytes 2949124
  5.3 4.5 %copy-start.8 = (bf16[32,1,1024,64]{2,3,1,0:T(8,128)(2,1)S(1)}, bf16[32,1,1024,64]{2,3,1,0:T(8,128)(2,1)}, u32[]{:S(2)}) copy-start(bf16[32,1,1024,64]{2,3,1,0:T(8,128)(2,1)} %param.18) | copy-start | bytes 12582916
  11.3 1.8 %copy-start.6 = (bf16[48,40]{0,1:T(8,128)(2,1)S(1)}, bf16[48,40]{0,1:T(8,128)(2,1)}, u32[]{:S(2)}) copy-start(bf16[48,40]{0,1:T(8,128)(2,1)} %param.21) | copy-start | bytes 11524
  14.4 25.4 %all-to-all-start = ((f32[32,1,2712]{2,1,0:T(1,128)}), f32[32,1,2712]{2,1,0:T(1,128)S(1)}, u32[]{:S(2)}, u32[]{:S(2)}) async-start(f32[32,1,2712]{2,1,0:T(1,128)} %all_to_all.23), calls=%async_computation | async-start | bytes 720896 | tf_op jit(solution)/shard_map/gather_partials/all_to_all | solution.py:99
  26.9 14.6 %copy-start.2 = (bf16[1,192,1536]{2,1,0:T(8,128)(2,1)S(1)}, bf16[1,192,1536]{2,1,0:T(8,128)(2,1)}, u32[]{:S(2)}) copy-start(bf16[1,192,1536]{2,1,0:T(8,128)(2,1)} %param.19) | copy-start | bytes 1769476
  39.8 4.1 %copy-start.5 = (s32[128,8]{0,1:T(8,128)S(1)}, s32[128,8]{0,1:T(8,128)}, u32[]{:S(2)}) copy-start(s32[128,8]{0,1:T(8,128)} %param.14) | copy-start | bytes 12292
  40.4 10.1 %copy-start.1 = (bf16[32,4,1536]{2,1,0:T(4,128)(2,1)S(1)}, bf16[32,4,1536]{2,1,0:T(4,128)(2,1)}, u32[]{:S(2)}) copy-start(bf16[32,4,1536]{2,1,0:T(4,128)(2,1)} %param.12) | copy-start | bytes 1179652
  41.7 3.1 %collective-permute-start = (f32[4,1536]{1,0:T(4,128)S(1)}, f32[4,1536]{1,0:T(4,128)S(1)}, u32[]{:S(2)}, u32[]{:S(2)}) collective-permute-start(f32[4,1536]{1,0:T(4,128)S(1)} %fusion.28), channel_id=1, source_target_pairs={{0,1},{1,0},{2,3},{3,2},{4,5},{5,4},{6,7},{7,6},{8,9},{9,8},{10,11... | collective-permute-start | bytes 73736 | tf_op jit(solution)/shard_map/sum_heads/ppermute | solution.py:26
  44.8 7.3 %copy-start.7 = (f32[1536]{0:T(1024)S(1)}, f32[1536]{0:T(1024)}, u32[]{:S(2)}) copy-start(f32[1536]{0:T(1024)} %param.20) | copy-start | bytes 18436
  44.8 2.8 %collective-permute-start.1 = (f32[4,1536]{1,0:T(4,128)S(1)}, f32[4,1536]{1,0:T(4,128)S(1)}, u32[]{:S(2)}, u32[]{:S(2)}) collective-permute-start(f32[4,1536]{1,0:T(4,128)S(1)} %add.136), channel_id=1, source_target_pairs={{0,2},{1,3},{2,0},{3,1},{4,6},{5,7},{6,4},{7,5},{8,10},{9,11},{10,... | collective-permute-start | bytes 73736 | tf_op jit(solution)/shard_map/sum_heads/ppermute | solution.py:26
  47.6 4.3 %collective-permute-start.2 = (f32[4,1536]{1,0:T(4,128)S(1)}, f32[4,1536]{1,0:T(4,128)S(1)}, u32[]{:S(2)}, u32[]{:S(2)}) collective-permute-start(f32[4,1536]{1,0:T(4,128)S(1)} %add.137), channel_id=1, source_target_pairs={{0,4},{1,5},{2,6},{3,7},{4,0},{5,1},{6,2},{7,3},{8,12},{9,13},{10,... | collective-permute-start | bytes 73736 | tf_op jit(solution)/shard_map/sum_heads/ppermute | solution.py:26
  50.6 16.4 %copy-start.3 = (bf16[5,48,2,512]{3,2,1,0:T(2,128)(2,1)S(1)}, bf16[5,48,2,512]{3,2,1,0:T(2,128)(2,1)}, u32[]{:S(2)}) copy-start(bf16[5,48,2,512]{3,2,1,0:T(2,128)(2,1)} %param.22) | copy-start | bytes 1474564
  53.5 13.4 %all-to-all-start.1 = ((f32[32,4,136]{2,1,0:T(4,128)}), f32[32,4,136]{2,1,0:T(4,128)S(1)}, u32[]{:S(2)}, u32[]{:S(2)}) async-start(f32[32,4,136]{2,1,0:T(4,128)} %pad_maximum_fusion.2), calls=%async_computation.1 | async-start | bytes 262144 | tf_op jit(solution)/shard_map/spread_rows/all_to_all | solution.py:162
  73.6 33.2 %all-to-all-start.2 = ((f32[32,1,10240]{2,1,0:T(1,128)}), f32[32,1,10240]{2,1,0:T(1,128)S(1)}, u32[]{:S(2)}, u32[]{:S(2)}) async-start(f32[32,1,10240]{2,1,0:T(1,128)} %all_to_all.31), calls=%async_computation.2 | async-start | bytes 2621440 | tf_op jit(solution)/shard_map/reduce_gate_up/all_to_all | solution.py:198
  107.6 20.6 %copy-start.4 = (bf16[5,48,512]{2,1,0:T(8,128)(2,1)S(1)}, bf16[5,48,512]{2,1,0:T(8,128)(2,1)}, u32[]{:S(2)}) copy-start(bf16[5,48,512]{2,1,0:T(8,128)(2,1)} %param.23) | copy-start | bytes 737284
  108.6 19.5 %all-to-all-start.3 = ((bf16[32,10,512]{2,1,0:T(8,128)(2,1)}), bf16[32,10,512]{2,1,0:T(8,128)(2,1)S(1)}, u32[]{:S(2)}, u32[]{:S(2)}) async-start(bf16[32,10,512]{2,1,0:T(8,128)(2,1)} %broadcast_in_dim.125), calls=%async_computation.3 | async-start | bytes 1048576 | tf_op jit(solution)/shard_map/gather_hidden/all_to_all | solution.py:206
  129.4 15.5 %all-to-all-start.4 = ((f32[8,1,768]{2,1,0:T(1,128)}), f32[8,1,768]{2,1,0:T(1,128)S(1)}, u32[]{:S(2)}, u32[]{:S(2)}) async-start(f32[8,1,768]{2,1,0:T(1,128)} %reshape.406), calls=%async_computation.4 | async-start | bytes 49152 | tf_op jit(solution)/shard_map/reduce_experts/all_to_all | solution.py:222

commit v2 on v1

--- a/solution.py
+++ b/solution.py
@@ -54,6 +54,11 @@
     tp_index = lax.axis_index("tp")
     own_request = seq_index * (requests // seq_size)
 
+    with jax.named_scope("gather_router"):
+        router_full = lax.all_to_all(
+            jnp.broadcast_to(w_router[None], (seq_size,) + w_router.shape), "seq", 0, 0, tiled=True
+        ).reshape(seq_size * part_width, -1)
+
     inputs = embedded.astype(jnp.float32)
     stat = jnp.mean(inputs * inputs, axis=-1, keepdims=True)
     normed = (inputs * lax.rsqrt(stat + EPSILON) * attn_gain).astype(jnp.bfloat16)
@@ -91,19 +96,9 @@
             preferred_element_type=jnp.float32,
         )
     partial = jnp.concatenate([sums, totals[..., None], local_top[..., None]], axis=-1)
-    partial = partial.reshape(seq_size, -1)
-    router_rows = jnp.broadcast_to(
-        w_router.astype(jnp.float32).reshape(1, -1), (seq_size, w_router.size)
-    )
+    partial = partial.reshape(seq_size, head_groups, new_count, head_extent + 2)
     with jax.named_scope("gather_partials"):
-        received = lax.all_to_all(
-            jnp.concatenate([partial, router_rows], axis=1), "seq", 0, 0, tiled=True
-        )
-    partial_size = partial.shape[1]
-    parts = received[:, :partial_size].reshape(seq_size, head_groups, new_count, head_extent + 2)
-    router_full = (
-        received[:, partial_size:].reshape(seq_size * part_width, -1).astype(jnp.bfloat16)
-    )
+        parts = lax.all_to_all(partial, "seq", 0, 0, tiled=True)
 
     with jax.named_scope("merge_request"):
         own_queries = lax.dynamic_index_in_dim(queries, own_request, 0, keepdims=False)[:, 0]
@@ -176,7 +171,8 @@
     before = jnp.dot(earlier, onehot, preferred_element_type=jnp.float32)
     slots = jnp.sum(before * onehot.astype(jnp.float32), axis=1).astype(jnp.int32)
     slots = slots.reshape(token_count, top_count)
-    picked = jnp.take_along_axis(logits, routes, axis=1)
+    choose = routes[:, :, None] == jnp.arange(expert_count, dtype=jnp.int32)[None, None, :]
+    picked = jnp.sum(jnp.where(choose, logits[:, None, :], 0.0), axis=-1)
     combine = jax.nn.softmax(picked, axis=-1)
     slot_ids = jnp.arange(capacity, dtype=jnp.int32)
     hits = (routes[None, None] == local_ids[:, None, None, None]) & (
@@ -193,10 +189,10 @@
     )
     slot_total = experts_here * capacity
     slots_each = slot_total // seq_size
-    both_part = both_part.reshape(seq_size, -1)
+    both_part = both_part.astype(jnp.bfloat16).reshape(seq_size, slots_each, -1)
     with jax.named_scope("reduce_gate_up"):
         both_pieces = lax.all_to_all(both_part, "seq", 0, 0, tiled=True)
-    both = jnp.sum(both_pieces, axis=0).reshape(slots_each, 2, -1)
+    both = jnp.sum(both_pieces.astype(jnp.float32), axis=0).reshape(slots_each, 2, -1)
     own_weight = lax.dynamic_slice_in_dim(
         slot_weight.reshape(-1), seq_index * slots_each, slots_each, 0
     )

time: 147 us -> 142 us (0.966)
  local copies, waits for them, and re-layouts: 21.2 us -> 9.66 us
  starting transfers between devices: 44 us -> 52.7 us
  waiting for transfers between devices: 61.3 us -> 59.2 us
    gather x5 -> x0, local copies, waits for them, and re-layouts: 7.39 us -> none  [per_device(): picked = jnp.take_along_axis(logits, routes, axis=1)]
    all_to_all x2 -> x1, local copies, waits for them, and re-layouts: 4.98 us -> 0.05 us  [per_device(): lax.all_to_all(jnp.broadcast_to(w_router[None], (seq_size,) + w_router.sh...]
    all_to_all x1, starting transfers between devices: 4.16 us -> 8.9 us  [per_device(): incoming = lax.all_to_all(outgoing, 'seq', 0, 0, tiled=True)]
    all_to_all x1 -> x2, starting transfers between devices: 12 us -> 16.6 us  [the longest x1 12 us: per_device(): parts = lax.all_to_all(partial, 'seq', 0, 0, tiled=True)]
    all_to_all x1 -> x2, waiting for transfers between devices: 12.6 us -> 8.09 us  [the longest x1 8.08 us: per_device(): parts = lax.all_to_all(partial, 'seq', 0, 0, tiled=True)]
    dot_general x1 -> x0, local copies, waits for them, and re-layouts: 2.08 us -> none  [per_device(): jnp.einsum('ecd,edgh->ecgh', expert_in, w_gate_up, preferred_element_type...]
    all_to_all x1, waiting for transfers between devices: 20.8 us -> 22.7 us  [per_device(): both_pieces = lax.all_to_all(both_part, 'seq', 0, 0, tiled=True)]
    unnamed x23 -> x25, local copies, waits for them, and re-layouts: 1.1 us -> 2.63 us
  transfers between devices with their start and end apart: 8 -> 9, of which waited for: 8 -> 8; matrix products, arithmetic and copies ran while one was open for 8% -> 5% of each run, Pallas kernels for 0% -> 0%
where the time goes in v2:
time: 142 us
  waiting for transfers between devices  59.2 us (42%)
  starting transfers between devices  52.7 us (37%)
  other arithmetic  12 us (8%)
  local copies, waits for them, and re-layouts  9.66 us (7%)
  matrix products  7.9 us (6%)
    all_to_all x1, waiting for transfers between devices, per_device(): both_pieces = lax.all_to_all(both_part, 'seq', 0, 0, tiled=True)  22.7 us
    all_to_all x1, waiting for transfers between devices, per_device(): lax.all_to_all(jnp.broadcast_to(hidden[None], (seq_size, slots_each, hid_...  12.5 us
    all_to_all x1, starting transfers between devices, per_device(): parts = lax.all_to_all(partial, 'seq', 0, 0, tiled=True)  12 us
    all_to_all x1, starting transfers between devices, per_device(): lax.all_to_all(moe_part.reshape(tp_size, row_count, part_width), 'tp', 0,...  10.9 us
    all_to_all x1, waiting for transfers between devices, per_device(): incoming = lax.all_to_all(outgoing, 'seq', 0, 0, tiled=True)  8.91 us
    all_to_all x1, starting transfers between devices, per_device(): incoming = lax.all_to_all(outgoing, 'seq', 0, 0, tiled=True)  8.9 us
    all_to_all x1, waiting for transfers between devices, per_device(): parts = lax.all_to_all(partial, 'seq', 0, 0, tiled=True)  8.08 us
    all_to_all x1, starting transfers between devices, per_device(): lax.all_to_all(jnp.broadcast_to(hidden[None], (seq_size, slots_each, hid_...  6.3 us
  transfers between devices with their start and end apart: 9, of which 8 were waited for; matrix products, arithmetic and copies ran while one was open for 5% of the time, Pallas kernels for 0%

profile of v2, /device:TPU:1, one launch (start us, length us, event | category | flops | bytes accessed | tf_op | source)
XLA Modules:
  0.0 141.9 jit_solution(10743075459070873555)
XLA Ops:
  0.0 0.7 convert_element_type.96
  0.8 1.3 multiply_reduce_fusion
  2.1 0.7 broadcast_compare_fusion
  3.1 1.3 fusion.31
  5.3 3.5 %fusion.80 = (f32[32,3,4]{2,1,0:T(4,128)S(1)}, f32[32,1,3,4,1024]{4,3,2,0,1:T(4,128)S(1)}) fusion(bf16[32,1,1024,64]{2,3,1,0:T(8,128)(2,1)} %param.17, bf16[32,4,3,64]{3,0,2,1:T(8,128)(2,1)S(1)} %pad_maximum_fusion.1, pred[32,1024]{1,0:T(8,128)(4,1)S(1)} %broadcast_compare_fusion), kind=kOutput, calls=%fused_computation.133 | convolution fusion | flops 51510912 | bytes 5850624 | tf_op jit(solution)/shard_map/cache_attention/rthqe,rhpe->rhqtp/dot_general | solution.py:83
  8.8 1.0 fusion.21
  9.8 1.5 %fusion.9 = f32[32,1,3,4,64]{4,3,2,0,1:T(4,128)S(1)} fusion(bf16[32,1,1024,64]{2,3,1,0:T(8,128)(2,1)S(1)} %copy-done.8, f32[32,1,3,4,1024]{4,3,2,0,1:T(4,128)S(1)} %get-tuple-element.21, f32[32,3,4]{2,1,0:T(4,128)S(1)} %get-tuple-element.20, pred[32,1024]{1,0:T(8,128)(4,1)S(1)} %broadcast_compare_fusion), kind=kOutput, calls=%fused_computation.15 | convolution fusion | flops 51511296 | bytes 5899776 | tf_op jit(solution)/shard_map/cache_attention/rhqtp,rhpe->rhqte/dot_general | solution.py:92
  11.3 0.7 copy.191
  12.0 0.7 copy.192
  12.7 1.0 maximum_bitcast_fusion
  13.7 12.0 %all-to-all-start = ((f32[32,3,4,66]{3,2,1,0:T(4,128)}), f32[32,3,4,66]{3,2,1,0:T(4,128)S(1)}, u32[]{:S(2)}, u32[]{:S(2)}) async-start(f32[32,3,4,66]{3,2,1,0:T(4,128)} %maximum_bitcast_fusion), calls=%async_computation | async-start | bytes 393216 | tf_op jit(solution)/shard_map/gather_partials/all_to_all | solution.py:101
  26.2 1.1 reshape.383
  27.6 8.1 %all-to-all-done = f32[32,3,4,66]{3,2,1,0:T(4,128)S(1)} async-done(((f32[32,3,4,66]{3,2,1,0:T(4,128)}), f32[32,3,4,66]{3,2,1,0:T(4,128)S(1)}, u32[]{:S(2)}, u32[]{:S(2)}) %all-to-all-start) | async-done | bytes 101408 | tf_op jit(solution)/shard_map/gather_partials/all_to_all | solution.py:101
  35.7 4.6 %all-to-all-start.1 = ((bf16[32,2,960]{2,1,0:T(2,128)(2,1)}), bf16[32,2,960]{2,1,0:T(2,128)(2,1)S(1)}, u32[]{:S(2)}, u32[]{:S(2)}) async-start(bf16[32,2,960]{2,1,0:T(2,128)(2,1)} %reshape.383), calls=%async_computation.1 | async-start | bytes 262144 | tf_op jit(solution)/shard_map/gather_router/all_to_all | solution.py:58
  42.0 1.9 %collective-permute-start = (f32[4,1536]{1,0:T(4,128)S(1)}, f32[4,1536]{1,0:T(4,128)S(1)}, u32[]{:S(2)}, u32[]{:S(2)}) collective-permute-start(f32[4,1536]{1,0:T(4,128)S(1)} %fusion.28), channel_id=1, source_target_pairs={{0,1},{1,0},{2,3},{3,2},{4,5},{5,4},{6,7},{7,6},{8,9},{9,8},{10,11... | collective-permute-start | bytes 73736 | tf_op jit(solution)/shard_map/sum_heads/ppermute | solution.py:26
  44.7 1.3 collective-permute-start.1
  46.7 1.1 collective-permute-done.1
  47.8 2.8 %collective-permute-start.2 = (f32[4,1536]{1,0:T(4,128)S(1)}, f32[4,1536]{1,0:T(4,128)S(1)}, u32[]{:S(2)}, u32[]{:S(2)}) collective-permute-start(f32[4,1536]{1,0:T(4,128)S(1)} %add.129), channel_id=1, source_target_pairs={{0,4},{1,5},{2,6},{3,7},{4,0},{5,1},{6,2},{7,3},{8,12},{9,13},{10,... | collective-permute-start | bytes 73736 | tf_op jit(solution)/shard_map/sum_heads/ppermute | solution.py:26
  53.1 0.8 pad_maximum_fusion
  53.9 8.9 %all-to-all-start.2 = ((f32[32,4,136]{2,1,0:T(4,128)}), f32[32,4,136]{2,1,0:T(4,128)S(1)}, u32[]{:S(2)}, u32[]{:S(2)}) async-start(f32[32,4,136]{2,1,0:T(4,128)} %pad_maximum_fusion), calls=%async_computation.2 | async-start | bytes 262144 | tf_op jit(solution)/shard_map/spread_rows/all_to_all | solution.py:157
  63.4 8.9 %all-to-all-done.2 = f32[32,4,136]{2,1,0:T(4,128)S(1)} async-done(((f32[32,4,136]{2,1,0:T(4,128)}), f32[32,4,136]{2,1,0:T(4,128)S(1)}, u32[]{:S(2)}, u32[]{:S(2)}) %all-to-all-start.2) | async-done | bytes 69664 | tf_op jit(solution)/shard_map/spread_rows/all_to_all | solution.py:157
  73.6 1.4 %reshape.366 = bf16[32,10,1024]{2,1,0:T(8,128)(2,1)} reshape(bf16[5,64,2,512]{3,2,1,0:T(2,128)(2,1)S(1)} %copy.209) | data formatting | bytes 1310720 | tf_op jit(solution)/shard_map/reshape | solution.py:192
  75.0 3.9 %all-to-all-start.3 = ((bf16[32,10,1024]{2,1,0:T(8,128)(2,1)}), bf16[32,10,1024]{2,1,0:T(8,128)(2,1)S(1)}, u32[]{:S(2)}, u32[]{:S(2)}) async-start(bf16[32,10,1024]{2,1,0:T(8,128)(2,1)} %reshape.366), calls=%async_computation.3 | async-start | bytes 2097152 | tf_op jit(solution)/shard_map/reduce_gate_up/all_to_all | solution.py:194
  79.2 0.7 fusion.8
  80.0 22.7 %all-to-all-done.3 = bf16[32,10,1024]{2,1,0:T(8,128)(2,1)S(1)} async-done(((bf16[32,10,1024]{2,1,0:T(8,128)(2,1)}), bf16[32,10,1024]{2,1,0:T(8,128)(2,1)S(1)}, u32[]{:S(2)}, u32[]{:S(2)}) %all-to-all-start.3) | async-done | bytes 655392 | tf_op jit(solution)/shard_map/reduce_gate_up/all_to_all | solution.py:194
  103.1 0.9 broadcast_in_dim.133
  103.9 6.3 %all-to-all-start.4 = ((bf16[32,10,512]{2,1,0:T(8,128)(2,1)}), bf16[32,10,512]{2,1,0:T(8,128)(2,1)S(1)}, u32[]{:S(2)}, u32[]{:S(2)}) async-start(bf16[32,10,512]{2,1,0:T(8,128)(2,1)} %broadcast_in_dim.133), calls=%async_computation.4 | async-start | bytes 1048576 | tf_op jit(solution)/shard_map/gather_hidden/all_to_all | solution.py:202
  110.5 12.5 %all-to-all-done.4 = bf16[32,10,512]{2,1,0:T(8,128)(2,1)S(1)} async-done(((bf16[32,10,512]{2,1,0:T(8,128)(2,1)}), bf16[32,10,512]{2,1,0:T(8,128)(2,1)S(1)}, u32[]{:S(2)}, u32[]{:S(2)}) %all-to-all-start.4) | async-done | bytes 327712 | tf_op jit(solution)/shard_map/gather_hidden/all_to_all | solution.py:202
  123.6 0.7 reshape.385
  124.3 10.9 %all-to-all-start.5 = ((f32[8,1,768]{2,1,0:T(1,128)}), f32[8,1,768]{2,1,0:T(1,128)S(1)}, u32[]{:S(2)}, u32[]{:S(2)}) async-start(f32[8,1,768]{2,1,0:T(1,128)} %reshape.385), calls=%async_computation.5 | async-start | bytes 49152 | tf_op jit(solution)/shard_map/reduce_experts/all_to_all | solution.py:218
  135.4 4.6 %all-to-all-done.5 = f32[8,1,768]{2,1,0:T(1,128)S(1)} async-done(((f32[8,1,768]{2,1,0:T(1,128)}), f32[8,1,768]{2,1,0:T(1,128)S(1)}, u32[]{:S(2)}, u32[]{:S(2)}) %all-to-all-start.5) | async-done | bytes 24608 | tf_op jit(solution)/shard_map/reduce_experts/all_to_all | solution.py:218
  140.5 0.7 reduce.3
  (100 shorter events, 12.2 us)
Async XLA Ops:
  0.0 4.4 %copy-start = (bf16[1536,1,320]{0,2,1:T(8,128)(2,1)S(1)}, bf16[1536,1,320]{0,2,1:T(8,128)(2,1)}, u32[]{:S(2)}) copy-start(bf16[1536,1,320]{0,2,1:T(8,128)(2,1)} %param.16) | copy-start | bytes 2949124
  5.3 4.5 %copy-start.8 = (bf16[32,1,1024,64]{2,3,1,0:T(8,128)(2,1)S(1)}, bf16[32,1,1024,64]{2,3,1,0:T(8,128)(2,1)}, u32[]{:S(2)}) copy-start(bf16[32,1,1024,64]{2,3,1,0:T(8,128)(2,1)} %param.18) | copy-start | bytes 12582916
  11.3 14.8 %copy-start.6 = (bf16[48,40]{0,1:T(8,128)(2,1)S(1)}, bf16[48,40]{0,1:T(8,128)(2,1)}, u32[]{:S(2)}) copy-start(bf16[48,40]{0,1:T(8,128)(2,1)} %param.21) | copy-start | bytes 11524
  13.7 22.0 %all-to-all-start = ((f32[32,3,4,66]{3,2,1,0:T(4,128)}), f32[32,3,4,66]{3,2,1,0:T(4,128)S(1)}, u32[]{:S(2)}, u32[]{:S(2)}) async-start(f32[32,3,4,66]{3,2,1,0:T(4,128)} %maximum_bitcast_fusion), calls=%async_computation | async-start | bytes 393216 | tf_op jit(solution)/shard_map/gather_partials/all_to_all | solution.py:101
  25.8 16.0 %copy-start.2 = (bf16[1,192,1536]{2,1,0:T(8,128)(2,1)S(1)}, bf16[1,192,1536]{2,1,0:T(8,128)(2,1)}, u32[]{:S(2)}) copy-start(bf16[1,192,1536]{2,1,0:T(8,128)(2,1)} %param.19) | copy-start | bytes 1769476
  26.2 17.6 %copy-start.5 = (s32[128,8]{0,1:T(8,128)S(1)}, s32[128,8]{0,1:T(8,128)}, u32[]{:S(2)}) copy-start(s32[128,8]{0,1:T(8,128)} %param.14) | copy-start | bytes 12292
  35.7 15.1 %all-to-all-start.1 = ((bf16[32,2,960]{2,1,0:T(2,128)(2,1)}), bf16[32,2,960]{2,1,0:T(2,128)(2,1)S(1)}, u32[]{:S(2)}, u32[]{:S(2)}) async-start(bf16[32,2,960]{2,1,0:T(2,128)(2,1)} %reshape.383), calls=%async_computation.1 | async-start | bytes 262144 | tf_op jit(solution)/shard_map/gather_router/all_to_all | solution.py:58
  40.6 10.0 %copy-start.1 = (bf16[32,4,1536]{2,1,0:T(4,128)(2,1)S(1)}, bf16[32,4,1536]{2,1,0:T(4,128)(2,1)}, u32[]{:S(2)}) copy-start(bf16[32,4,1536]{2,1,0:T(4,128)(2,1)} %param.12) | copy-start | bytes 1179652
  42.0 2.7 %collective-permute-start = (f32[4,1536]{1,0:T(4,128)S(1)}, f32[4,1536]{1,0:T(4,128)S(1)}, u32[]{:S(2)}, u32[]{:S(2)}) collective-permute-start(f32[4,1536]{1,0:T(4,128)S(1)} %fusion.28), channel_id=1, source_target_pairs={{0,1},{1,0},{2,3},{3,2},{4,5},{5,4},{6,7},{7,6},{8,9},{9,8},{10,11... | collective-permute-start | bytes 73736 | tf_op jit(solution)/shard_map/sum_heads/ppermute | solution.py:26
  44.7 3.1 %collective-permute-start.1 = (f32[4,1536]{1,0:T(4,128)S(1)}, f32[4,1536]{1,0:T(4,128)S(1)}, u32[]{:S(2)}, u32[]{:S(2)}) collective-permute-start(f32[4,1536]{1,0:T(4,128)S(1)} %add.128), channel_id=1, source_target_pairs={{0,2},{1,3},{2,0},{3,1},{4,6},{5,7},{6,4},{7,5},{8,10},{9,11},{10,... | collective-permute-start | bytes 73736 | tf_op jit(solution)/shard_map/sum_heads/ppermute | solution.py:26
  46.6 5.9 %copy-start.7 = (f32[1536]{0:T(1024)S(1)}, f32[1536]{0:T(1024)}, u32[]{:S(2)}) copy-start(f32[1536]{0:T(1024)} %param.20) | copy-start | bytes 18436
  47.8 4.6 %collective-permute-start.2 = (f32[4,1536]{1,0:T(4,128)S(1)}, f32[4,1536]{1,0:T(4,128)S(1)}, u32[]{:S(2)}, u32[]{:S(2)}) collective-permute-start(f32[4,1536]{1,0:T(4,128)S(1)} %add.129), channel_id=1, source_target_pairs={{0,4},{1,5},{2,6},{3,7},{4,0},{5,1},{6,2},{7,3},{8,12},{9,13},{10,... | collective-permute-start | bytes 73736 | tf_op jit(solution)/shard_map/sum_heads/ppermute | solution.py:26
  50.7 21.6 %copy-start.3 = (bf16[5,48,2,512]{3,2,1,0:T(2,128)(2,1)S(1)}, bf16[5,48,2,512]{3,2,1,0:T(2,128)(2,1)}, u32[]{:S(2)}) copy-start(bf16[5,48,2,512]{3,2,1,0:T(2,128)(2,1)} %param.22) | copy-start | bytes 1474564
  53.9 18.4 %all-to-all-start.2 = ((f32[32,4,136]{2,1,0:T(4,128)}), f32[32,4,136]{2,1,0:T(4,128)S(1)}, u32[]{:S(2)}, u32[]{:S(2)}) async-start(f32[32,4,136]{2,1,0:T(4,128)} %pad_maximum_fusion), calls=%async_computation.2 | async-start | bytes 262144 | tf_op jit(solution)/shard_map/spread_rows/all_to_all | solution.py:157
  75.0 27.7 %all-to-all-start.3 = ((bf16[32,10,1024]{2,1,0:T(8,128)(2,1)}), bf16[32,10,1024]{2,1,0:T(8,128)(2,1)S(1)}, u32[]{:S(2)}, u32[]{:S(2)}) async-start(bf16[32,10,1024]{2,1,0:T(8,128)(2,1)} %reshape.366), calls=%async_computation.3 | async-start | bytes 2097152 | tf_op jit(solution)/shard_map/reduce_gate_up/all_to_all | solution.py:194
  102.9 20.2 %copy-start.4 = (bf16[5,48,512]{2,1,0:T(8,128)(2,1)S(1)}, bf16[5,48,512]{2,1,0:T(8,128)(2,1)}, u32[]{:S(2)}) copy-start(bf16[5,48,512]{2,1,0:T(8,128)(2,1)} %param.23) | copy-start | bytes 737284
  103.9 19.0 %all-to-all-start.4 = ((bf16[32,10,512]{2,1,0:T(8,128)(2,1)}), bf16[32,10,512]{2,1,0:T(8,128)(2,1)S(1)}, u32[]{:S(2)}, u32[]{:S(2)}) async-start(bf16[32,10,512]{2,1,0:T(8,128)(2,1)} %broadcast_in_dim.133), calls=%async_computation.4 | async-start | bytes 1048576 | tf_op jit(solution)/shard_map/gather_hidden/all_to_all | solution.py:202
  124.3 15.6 %all-to-all-start.5 = ((f32[8,1,768]{2,1,0:T(1,128)}), f32[8,1,768]{2,1,0:T(1,128)S(1)}, u32[]{:S(2)}, u32[]{:S(2)}) async-start(f32[8,1,768]{2,1,0:T(1,128)} %reshape.385), calls=%async_computation.5 | async-start | bytes 49152 | tf_op jit(solution)/shard_map/reduce_experts/all_to_all | solution.py:218
